TPU v7x, 256 devices: a whole 4x4x8 slice. The times are simulated.
256 devices in a mesh: wall: 8 (over y_lo, x), stream: 32 (over z, y_hi, core).
Axes of the slice: x: 4, y: 4 (y_hi: 2, y_lo: 2; y = y_hi * 2 + y_lo), z: 8, core: 2. Of those that a mesh axis runs over, the one named last changes fastest.
Arguments:
- velocity: float32 [3, 64, 512, 128], P(None, 'wall', 'stream'), may hold values from -6 to 6
- sample_block: int32 [8, 256], P('wall', 'stream'), may hold values from 0 to 127
- sample_member: int32 [8, 256, 1], P('wall', 'stream'), may hold values from 0 to 7; in each aligned block of 8 rows (0 to 7, 8 to 15, ..., all dimensions but the last counted through in order) at most 2 rows name the same one
- k_first: bfloat16 [8, 54, 64], P('wall'), may hold values from -6 to 6
- k_second: bfloat16 [8, 27, 64, 64], P('wall'), may hold values from -6 to 6
- w_hidden: bfloat16 [8, 2048, 2048], P('wall'), may hold values from -6 to 6
- w_out: bfloat16 [8, 2048, 2], P('wall'), may hold values from -6 to 6
Outputs:
- new_field: float32 [3, 64, 512, 128], P(None, 'wall', 'stream')
- stress: float32 [2, 8, 256], P(None, 'wall', 'stream')
- new_k_first: float32 [8, 54, 64], P('wall')
- new_k_second: float32 [8, 27, 64, 64], P('wall')
- new_w_hidden: float32 [8, 2048, 2048], P('wall', 'stream')
- new_w_out: float32 [8, 2048, 2], P('wall')
Inputs may be any that keep to these rules, and one draw needn't show every extreme that they name: `sample_member`: in the list of one slab at most 2 samples name the same member; in every draw some slab names some member exactly 2 times.
All inputs are finite; a program needn't handle non-finite values.
Results may differ from a plain program's by a relative error of at most 0.0064.
Values may be sent and summed in bfloat16 or wider, within the bound.
No kernel may reach another device: no remote copies, remote signals or barrier semaphores. Data moves between devices by JAX's collectives and lax.ppermute only.
A program may use at most 128 MiB of HBM per device.

v0:
```python
import math
import jax
import jax.numpy as jnp
import numpy as np
from jax import lax
from jax.sharding import Mesh
from jax.sharding import PartitionSpec as P

P_SIZE = 8
PY = 4
PX = 4
PZ = 8
CH = 64
CAP = 2
FEATS = 2048
STREAM = ("stream_0", "stream_1", "stream_2")
highest = lax.Precision.HIGHEST
time_step = 0.005
relax_rate = 20.0
viscosity = 0.3
learn_rate = 0.5
rms_eps = 1e-06


def extended(shard, sides, width):
    edges = {}
    for axis, dim in sides:
        size, length = (lax.axis_size(axis), shard.shape[dim])
        up = [(i, (i + 1) % size) for i in range(size)]
        last = lax.slice_in_dim(shard, length - width, length, axis=dim)
        first = lax.slice_in_dim(shard, 0, width, axis=dim)
        edges[dim] = (
            lax.ppermute(last, axis, up),
            lax.ppermute(first, axis, [(b, a) for a, b in up]),
        )
    done = []
    for _, dim in sides:
        low, high = edges[dim]
        around = [(width, width) if d in done else (0, 0) for d in range(shard.ndim)]
        shard = jnp.concatenate([jnp.pad(low, around), shard, jnp.pad(high, around)], axis=dim)
        done.append(dim)
    return shard


def in_one_piece(arrays, axis, split_dim, concat_dim, along):
    widths = [math.prod(a.shape[along:]) for a in arrays]
    both = jnp.concatenate(
        [a.reshape(*a.shape[:along], w) for a, w in zip(arrays, widths)], axis=along
    )
    whole = lax.all_to_all(both, axis, split_axis=split_dim, concat_axis=concat_dim, tiled=True)
    tiles = jnp.split(whole, [sum(widths[:k]) for k in range(1, len(widths))], axis=along)
    return tuple((b.reshape(*whole.shape[:along], *a.shape[along:]) for a, b in zip(arrays, tiles)))


def joined_along(tiles, dim):
    lengths = list(tiles.shape[1:])
    lengths[dim] *= tiles.shape[0]
    return jnp.moveaxis(tiles, 0, dim).reshape(lengths)


def gather_in_order(shard, axes, order):
    tiles = shard
    for k in order:
        tiles = lax.all_gather(tiles, axes[k])
    done = order[::-1]
    back = [done.index(k) for k in range(len(axes))]
    tiles = tiles.transpose(*back, *range(len(axes), tiles.ndim))
    return tiles.reshape(-1, *shard.shape)


def gathered_by_axis(shard, axes, order, dim):
    return joined_along(gather_in_order(shard, axes, order), dim)


def cheb_tables(points):
    order = points - 1
    node_index = np.arange(points)
    nodes = -np.cos(np.pi * node_index / order)
    end_weight = np.where((node_index == 0) | (node_index == order), 2.0, 1.0)
    parity = (-1.0) ** (node_index[:, None] + node_index[None, :])
    offdiag = 1.0 - np.eye(points)
    spread = nodes[:, None] - nodes[None, :] + np.eye(points)
    deriv = end_weight[:, None] / end_weight[None, :] * parity / spread * offdiag
    deriv = deriv - np.eye(points) * deriv.sum(axis=1)[:, None]
    highpass = parity / (order * end_weight[None, :])
    return (deriv, highpass, 0.5 * order * order)


def axis_matrices(count, periodic):
    deriv, highpass, lift_half = cheb_tables(P_SIZE)
    length = count * P_SIZE
    slope = np.kron(np.eye(count), deriv)
    upper = np.kron(np.eye(count), highpass)
    faces = count if periodic else count - 1
    for element in range(faces):
        last_node = element * P_SIZE + P_SIZE - 1
        next_node = (element + 1) % count * P_SIZE
        slope[last_node, next_node] += lift_half
        slope[last_node, last_node] -= lift_half
        slope[next_node, last_node] -= lift_half
        slope[next_node, next_node] += lift_half
    if not periodic:
        slope[0, 0] += lift_half
        slope[length - 1, length - 1] -= lift_half
    paired = jnp.asarray(np.concatenate([slope, upper], axis=0), jnp.float32)
    return (paired, lift_half)


def slot_matrix(members, member_count):
    member_hot = (members[..., None] == jnp.arange(member_count, dtype=jnp.int32)).astype(jnp.int32)
    before = jnp.cumsum(member_hot, axis=-2) - member_hot
    ranks = jnp.sum(before * member_hot, axis=-1)
    slots = members * CAP + ranks
    return (slots[..., None, :] == jnp.arange(member_count * CAP, dtype=jnp.int32)[:, None]).astype(
        jnp.float32
    )


DIMS = ("NDHWC", "DHWIO", "NDHWC")
FILTER_DIMS = ("CDHWN", "IDHWO", "NDHWC")
SAME = ((1, 1), (1, 1), (1, 1))


def silu_slope(value):
    gate = jax.nn.sigmoid(value)
    return gate * (1.0 + value * (1.0 - gate))


def conv_taps(grid, kernel):
    return lax.conv_general_dilated(
        grid, kernel, (1, 1, 1), SAME, dimension_numbers=DIMS, preferred_element_type=jnp.float32
    )


def conv_filter(grid, delta):
    taps = lax.conv_general_dilated(
        grid,
        delta,
        (1, 1, 1),
        SAME,
        dimension_numbers=FILTER_DIMS,
        preferred_element_type=jnp.float32,
    )
    return jnp.moveaxis(taps, 0, 3)


def forward_back(patches, aim_rows, valid, k_first, k_second, w_hidden, w_out):
    batch = patches.shape[0]
    channels = k_second.shape[-1]
    inputs = patches.reshape(batch, 2, PY, PX, PZ).transpose(0, 2, 3, 4, 1)
    first_taps = k_first.reshape(3, 3, 3, 2, channels)
    second_taps = k_second.reshape(3, 3, 3, channels, channels)
    scale_one = 1.0 / math.sqrt(54.0)
    scale_two = 1.0 / math.sqrt(27.0 * channels)
    scale_three = 1.0 / math.sqrt(1.0 * w_hidden.shape[0])
    scale_four = 1.0 / math.sqrt(1.0 * w_hidden.shape[1])
    pre_one = conv_taps(inputs, first_taps) * scale_one
    hidden_one = jax.nn.silu(pre_one).astype(jnp.bfloat16)
    pre_two = conv_taps(hidden_one, second_taps) * scale_two
    pooled = (
        jax.nn.silu(pre_two).reshape(batch, PY // 2, 2, PX // 2, 2, PZ, channels).mean(axis=(2, 4))
    )
    features = pooled.reshape(batch, -1).astype(jnp.bfloat16)
    pre_three = jnp.dot(features, w_hidden, preferred_element_type=jnp.float32) * scale_three
    hidden_three = jax.nn.silu(pre_three).astype(jnp.bfloat16)
    pred = jnp.dot(hidden_three, w_out, preferred_element_type=jnp.float32) * scale_four
    error = valid.astype(jnp.float32)[:, None] * (pred - aim_rows.astype(jnp.float32))
    grad_out = jnp.dot(hidden_three.astype(jnp.float32).T, error, precision=highest) * scale_four
    delta_three = (
        jnp.dot(error, w_out.astype(jnp.float32).T, precision=highest)
        * scale_four
        * silu_slope(pre_three)
    ).astype(jnp.bfloat16)
    back_feat = jnp.dot(delta_three, w_hidden.T, preferred_element_type=jnp.float32) * scale_three
    back_grid = back_feat.reshape(batch, PY // 2, 1, PX // 2, 1, PZ, channels)
    spread_back = (
        jnp.broadcast_to(back_grid, (batch, PY // 2, 2, PX // 2, 2, PZ, channels)).reshape(
            pre_two.shape
        )
        * 0.25
    )
    delta_two = (spread_back * silu_slope(pre_two)).astype(jnp.bfloat16)
    grad_two = (conv_filter(hidden_one, delta_two) * scale_two).reshape(27, channels, channels)
    mirrored = jnp.flip(second_taps, axis=(0, 1, 2)).swapaxes(3, 4)
    back_one = conv_taps(delta_two, mirrored)
    delta_one = (back_one * scale_two * silu_slope(pre_one)).astype(jnp.bfloat16)
    grad_one = (conv_filter(inputs, delta_one) * scale_one).reshape(54, channels)
    return (pred, grad_one, grad_two, grad_out, features, delta_three)


def row_update(weight, grad):
    scale = jnp.sqrt(jnp.mean(grad * grad, axis=-1, keepdims=True) + rms_eps)
    return weight.astype(jnp.float32) - learn_rate * grad / scale


def whole_update(weight, grad):
    scale = jnp.sqrt(jnp.mean(grad * grad) + rms_eps)
    return weight.astype(jnp.float32) - learn_rate * grad / scale


def body(velocity, sample_block, sample_member, k_first, k_second, w_hidden, w_out):
    wall_count = lax.axis_size("wall")
    wall_place = lax.axis_index("wall")
    flow_count = lax.axis_size(STREAM)
    flow_place = lax.axis_index(STREAM)
    padded = extended(velocity, (("wall", 1), (STREAM, 2)), 1)
    keep_low = (wall_place > 0).astype(jnp.float32)
    keep_high = (wall_place < wall_count - 1).astype(jnp.float32)
    below = padded[:, 0, 1:-1, :] * keep_low
    above = padded[:, -1, 1:-1, :] * keep_high
    left_face = padded[:, 1:-1, 0, :]
    right_face = padded[:, 1:-1, -1, :]
    size_y, size_x, size_z = (velocity.shape[1], velocity.shape[2], velocity.shape[3])
    pair_y, lift_half = axis_matrices(size_y // P_SIZE, False)
    pair_x, lift_same = axis_matrices(size_x // P_SIZE, False)
    pair_z, lift_again = axis_matrices(size_z // P_SIZE, True)
    along_y = jnp.einsum("cyxz,wy->cwxz", velocity, pair_y, precision=highest)
    grad_y = (
        along_y[:, :size_y]
        .at[:, 0]
        .add(-lift_half * below)
        .at[:, size_y - 1]
        .add(lift_half * above)
    )
    high_y = along_y[:, size_y:]
    along_x = jnp.einsum("cyxz,wx->cywz", velocity, pair_x, precision=highest)
    grad_x = (
        along_x[:, :, :size_x]
        .at[:, :, 0]
        .add(-lift_half * left_face)
        .at[:, :, size_x - 1]
        .add(lift_half * right_face)
    )
    high_x = along_x[:, :, size_x:]
    along_z = jnp.einsum("cyxz,wz->cyxw", velocity, pair_z, precision=highest)
    grad_z = along_z[..., :size_z]
    high_z = along_z[..., size_z:]
    advect = velocity[0][None] * grad_x + velocity[1][None] * grad_y + velocity[2][None] * grad_z
    new_field = velocity + time_step * (-advect - relax_rate * (high_x + high_y + high_z))
    rows_y, rows_x, rows_z = (size_y // PY, size_x // PX, size_z // PZ)
    tangent = jnp.stack([velocity[0], velocity[2]]).reshape(2, rows_y, PY, rows_x, PX, rows_z, PZ)
    blocks = tangent.transpose(1, 3, 5, 0, 2, 4, 6).reshape(-1, 2 * PY * PX * PZ)
    slope_wall = jnp.stack([grad_y[0], grad_y[2]]).reshape(2, rows_y, PY, rows_x, PX, rows_z, PZ)
    stress_true = (
        (viscosity * jnp.mean(slope_wall, axis=(2, 4, 6))).transpose(1, 2, 3, 0).reshape(-1, 2)
    )
    picked = sample_block.reshape(-1)
    members = sample_member.reshape(-1)
    patch_rows = jnp.take(blocks, picked, axis=0).astype(jnp.bfloat16)
    aim_rows = jnp.take(stress_true, picked, axis=0).astype(jnp.bfloat16)
    select = slot_matrix(members, wall_count)
    select_half = select.astype(jnp.bfloat16)
    send_rows = jnp.dot(select_half, patch_rows, preferred_element_type=jnp.float32).astype(
        jnp.bfloat16
    )
    send_aims = jnp.dot(select_half, aim_rows, preferred_element_type=jnp.float32).astype(
        jnp.bfloat16
    )
    send_valid = jnp.sum(select, axis=1).astype(jnp.bfloat16)
    recv_rows, recv_aims, recv_valid = in_one_piece(
        (send_rows, send_aims, send_valid), "wall", 0, 0, 1
    )
    pred, grad_one, grad_two, grad_out, features, delta_three = forward_back(
        recv_rows, recv_aims, recv_valid, k_first[0], k_second[0], w_hidden[0], w_out[0]
    )
    back = lax.all_to_all(pred, "wall", split_axis=0, concat_axis=0, tiled=True)
    stress_local = jnp.dot(select.T, back, precision=highest)
    stress = stress_local.T[:, None, :]
    share_rows = FEATS // flow_count
    dense_scale = 1.0 / math.sqrt(1.0 * FEATS)
    columns_here = lax.all_to_all(features, STREAM, split_axis=1, concat_axis=0, tiled=True)
    grad_hidden = (
        jnp.dot(
            columns_here.T,
            gathered_by_axis(delta_three, STREAM, (1, 0, 2), 0),
            preferred_element_type=jnp.float32,
        )
        * dense_scale
    )
    own_rows = lax.dynamic_slice_in_dim(w_hidden[0], flow_place * share_rows, share_rows, 0)
    new_w_hidden = row_update(own_rows, grad_hidden)[None]
    grad_one, grad_two, grad_out = lax.psum((grad_one, grad_two, grad_out), STREAM)
    new_k_second = row_update(k_second[0], grad_two)
    new_k_first = row_update(k_first[0], grad_one)
    new_w_out = whole_update(w_out[0], grad_out)
    return (new_field, stress, new_k_first[None], new_k_second[None], new_w_hidden, new_w_out[None])


def solution(mesh):
    torus = Mesh(
        mesh.devices.reshape(mesh.shape["wall"], 8, 2, 2),
        ("wall", "stream_0", "stream_1", "stream_2"),
    )
    in_specs = (
        P(None, "wall", STREAM, None),
        P("wall", STREAM),
        P("wall", STREAM, None),
        P("wall", None, None),
        P("wall", None, None, None),
        P("wall", None, None),
        P("wall", None, None),
    )
    out_specs = (
        P(None, "wall", STREAM, None),
        P(None, "wall", STREAM),
        P("wall", None, None),
        P("wall", None, None, None),
        P("wall", STREAM, None),
        P("wall", None, None),
    )
    return jax.shard_map(body, mesh=torus, in_specs=in_specs, out_specs=out_specs, check_vma=False)
```

profile of v0, /device:TPU:1, one launch (start us, length us, event | category | flops | bytes accessed | tf_op | source)
XLA Modules:
  0.0 358.8 jit_solution(1956748719228689826)
XLA Ops:
  8.8 2.0 collective-permute-start.2
  10.9 2.4 collective-permute-start.3
  13.2 1.6 fusion.46
  14.8 4.0 %collective-permute-start = (f32[3,8,1,128]{3,2,1,0:T(1,128)}, f32[3,8,1,128]{3,2,1,0:T(1,128)}, u32[]{:S(2)}, u32[]{:S(2)}) collective-permute-start(f32[3,8,1,128]{3,2,1,0:T(1,128)} %get-tuple-element.94), channel_id=1, source_target_pairs={{0,1},{1,2},{2,3},{3,4},{4,5},{5,6},{6,7},{7,8},{8,9},{9,10},{10,1... | collective-permute-start | bytes 36872 | tf_op jit(solution)/shard_map/ppermute | solution.py:33
  20.1 0.9 fusion.44
  21.0 1.5 convolution_bitcast_fusion
  22.5 1.5 fusion.23
  24.0 1.5 convolution_bitcast_fusion.1
  26.2 0.8 select_reduce_fusion
  27.7 1.2 reshape.297
  32.6 2.1 reshape.300
  35.6 0.9 convolution_convert_fusion.1
  37.3 3.3 all-to-all-start
  41.0 4.7 %all-to-all-done = bf16[8,2,259]{2,1,0:T(2,128)(2,1)S(1)} async-done(((bf16[8,2,259]{2,1,0:T(2,128)(2,1)}), bf16[8,2,259]{2,1,0:T(2,128)(2,1)S(1)}, u32[]{:S(2)}, u32[]{:S(2)}) %all-to-all-start) | async-done | bytes 8320 | tf_op jit(solution)/shard_map/all_to_all | solution.py:50
  46.0 0.9 convolution_multiply_fusion.4
  46.9 4.5 %fusion.14 = (f32[16,4,4,8,64]{4,0,3,2,1:T(8,128)}, f32[16,4,4,8,64]{4,0,3,2,1:T(8,128)}) fusion(bf16[3,3,3,64,64]{4,3,2,1,0:T(8,128)(2,1)} %bitcast.138, f32[16,4,4,8,64]{4,0,3,2,1:T(8,128)S(1)} %convolution_multiply_fusion.4), kind=kOutput, calls=%fused_computation.26 | convolution fusion | flops 289669120 | bytes 1794048 | tf_op jit(solution)/shard_map/conv_general_dilated | solution.py:130
  51.4 1.3 reduce_sum.75
  53.1 4.6 %multiply_convert_fusion.3 = (bf16[16,2048]{1,0:T(8,128)(2,1)S(1)}, f32[16,2048]{1,0:T(8,128)S(1)}) fusion(bf16[16,2048]{1,0:T(8,128)(2,1)S(1)} %convert_element_type.116, bf16[1,2048,2048]{2,1,0:T(8,128)(2,1)} %param.23), kind=kOutput, calls=%fused_computation.50 | convolution fusion | flops 134414336 | bytes 8650752 | tf_op jit(solution)/shard_map/dot_general | solution.py:164
  58.6 5.4 %all-gather = bf16[32,2048]{1,0:T(8,128)(2,1)} all-gather(bf16[16,2048]{1,0:T(8,128)(2,1)S(1)} %fusion.11), channel_id=2, replica_groups=mesh['wall'=8,'stream_0'=8,'stream_1'=2,'stream_2'=2] {'stream_1'}, dimensions={0}, use_global_device_ids=true | all-gather | bytes 196608 | tf_op jit(solution)/shard_map/all_gather | solution.py:64
  66.6 5.7 %fusion.8 = f32[16,2048]{1,0:T(8,128)S(1)} fusion(bf16[16,2048]{1,0:T(8,128)(2,1)S(1)} %fusion.11, bf16[1,2048,2048]{2,1,0:T(8,128)(2,1)} %param.23), kind=kOutput, calls=%fused_computation.9 | convolution fusion | flops 134250496 | bytes 8585216 | tf_op jit(solution)/shard_map/dot_general | solution.py:174
  73.1 3.6 %convolution_multiply_fusion.5 = f32[3,3,3,64,64]{4,3,2,1,0:T(8,128)} fusion(bf16[16,4,4,8,64]{4,0,3,2,1:T(8,128)(2,1)S(1)} %multiply_convert_fusion, f32[16,4,4,8,64]{4,0,3,2,1:T(8,128)S(1)} %convolution_multiply_fusion.4), kind=kOutput, calls=%fused_computation.16 | convolution fusion | flops 289124352 | bytes 1228800 | tf_op jit(solution)/shard_map/transpose | solution.py:144
  77.1 4.2 %convolution_multiply_fusion.6 = f32[3,3,3,2,64]{4,3,2,1,0:T(2,128)S(1)} fusion(bf16[16,2,4,4,8]{0,4,3,2,1:T(8,128)(2,1)S(1)} %bitcast.141, bf16[16,4,4,8,64]{4,0,3,2,1:T(8,128)(2,1)S(1)} %multiply_convert_fusion, bf16[3,3,3,64,64]{4,3,2,1,0:T(8,128)(2,1)S(1)} %bitcast.139, f32[16,4,4,8,64]{4,0,3,2,1:T(8,128)S(1)} %convolution_multiply_fusion.4), kind=kOutput, calls=%fused_computation.20 | convolution fusion | flops 298683776 | bytes 1029632 | tf_op jit(solution)/shard_map/transpose | solution.py:144
  81.3 19.8 %all-gather.6.cloned.1.call-done = bf16[16,16,2048]{2,1,0:T(8,128)(2,1)} async-done(((bf16[2,16,2048]{2,1,0:T(8,128)(2,1)}), bf16[16,16,2048]{2,1,0:T(8,128)(2,1)}) %all-gather.6.cloned.1.call-update) | async-done | bytes 1048592 | tf_op jit(solution)/shard_map/all_gather | solution.py:64
  102.0 4.9 %all-to-all-start.1 = ((f32[8,2,2]{1,2,0:T(2,128)}), f32[8,2,2]{1,2,0:T(2,128)S(1)}, u32[]{:S(2)}, u32[]{:S(2)}) async-start(f32[8,2,2]{1,2,0:T(2,128)} %copy.77), calls=%async_computation.1 | async-start | bytes 16384 | tf_op jit(solution)/shard_map/all_to_all | solution.py:266
  107.0 128.6 %all-reduce = (f32[54,64]{1,0:T(8,128)S(1)}, f32[2048,2]{0,1:T(2,128)S(1)}) all-reduce(f32[54,64]{1,0:T(8,128)S(1)} %reshape.304, f32[2048,2]{0,1:T(2,128)S(1)} %convolution_multiply_fusion.1), channel_id=1, replica_groups=mesh['wall'=8,'stream_0'=8,'stream_1'=2,'stream_2'=2] {'stream_0','strea..., use_global_device_ids=true, to_apply=%region_5.6 | all-reduce | flops 7552 | bytes 60416 | tf_op jit(solution)/shard_map/psum | solution.py:282
  239.1 10.2 %all-to-all-start.2 = ((bf16[32,2,512]{2,1,0:T(2,128)(2,1)}), bf16[32,2,512]{2,1,0:T(2,128)(2,1)S(1)}, u32[]{:S(2)}, u32[]{:S(2)}) async-start(bf16[32,2,512]{2,1,0:T(2,128)(2,1)} %reshape.333), calls=%async_computation.2 | async-start | bytes 131072 | tf_op jit(solution)/shard_map/all_to_all | solution.py:271
  250.2 9.0 %all-to-all-done.2 = bf16[32,2,512]{2,1,0:T(2,128)(2,1)S(1)} async-done(((bf16[32,2,512]{2,1,0:T(2,128)(2,1)}), bf16[32,2,512]{2,1,0:T(2,128)(2,1)S(1)}, u32[]{:S(2)}, u32[]{:S(2)}) %all-to-all-start.2) | async-done | bytes 65568 | tf_op jit(solution)/shard_map/all_to_all | solution.py:271
  259.3 84.0 %all-reduce.3.cloned.1.call-done = f32[27,64,64]{2,1,0:T(8,128)} async-done(((f32[27,64,64]{2,1,0:T(8,128)}), f32[27,64,64]{2,1,0:T(8,128)}) %all-reduce.3.cloned.1.call-update) | async-done | bytes 442384 | tf_op jit(solution)/shard_map/psum | solution.py:282
  343.3 1.5 multiply_reduce_fusion
  344.7 2.4 fusion.15
  347.1 1.7 copy.82
  349.5 1.9 fusion.16
  (120 shorter events, 19.6 us)
Async XLA Ops:
  8.0 32.9 %copy-start = (f32[3,8,16,128]{3,2,1,0:T(8,128)S(1)}, f32[3,8,16,128]{3,2,1,0:T(8,128)}, u32[]{:S(2)}) copy-start(f32[3,8,16,128]{3,2,1,0:T(8,128)} %param.18) | copy-start | bytes 589828
  8.0 32.9 %copy-start.9 = (bf16[1,54,64]{2,1,0:T(8,128)(2,1)S(1)}, bf16[1,54,64]{2,1,0:T(8,128)(2,1)}, u32[]{:S(2)}) copy-start(bf16[1,54,64]{2,1,0:T(8,128)(2,1)} %param.21) | copy-start | bytes 20740
  8.8 22.3 %collective-permute-start.2 = (f32[3,1,16,128]{3,2,1,0:T(8,128)S(1)}, f32[3,1,16,128]{3,2,1,0:T(8,128)S(1)}, u32[]{:S(2)}, u32[]{:S(2)}) collective-permute-start(f32[3,1,16,128]{3,2,1,0:T(8,128)S(1)} %get-tuple-element.96), channel_id=1, source_target_pairs={{0,32},{32,64},{64,96},{96,128},{128,160},{160,192},{192,224},{224... | collective-permute-start | bytes 73736 | tf_op jit(solution)/shard_map/ppermute | solution.py:33
  10.9 20.3 %collective-permute-start.3 = (f32[3,1,16,128]{3,2,1,0:T(8,128)S(1)}, f32[3,1,16,128]{3,2,1,0:T(8,128)S(1)}, u32[]{:S(2)}, u32[]{:S(2)}) collective-permute-start(f32[3,1,16,128]{3,2,1,0:T(8,128)S(1)} %get-tuple-element.95), channel_id=1, source_target_pairs={{32,0},{64,32},{96,64},{128,96},{160,128},{192,160},{224,192},{0,2... | collective-permute-start | bytes 73736 | tf_op jit(solution)/shard_map/ppermute | solution.py:34
  14.8 49.3 %collective-permute-start = (f32[3,8,1,128]{3,2,1,0:T(1,128)}, f32[3,8,1,128]{3,2,1,0:T(1,128)}, u32[]{:S(2)}, u32[]{:S(2)}) collective-permute-start(f32[3,8,1,128]{3,2,1,0:T(1,128)} %get-tuple-element.94), channel_id=1, source_target_pairs={{0,1},{1,2},{2,3},{3,4},{4,5},{5,6},{6,7},{7,8},{8,9},{9,10},{10,1... | collective-permute-start | bytes 36872 | tf_op jit(solution)/shard_map/ppermute | solution.py:33
  18.8 46.1 %collective-permute-start.1 = (f32[3,8,1,128]{3,2,1,0:T(1,128)S(1)}, f32[3,8,1,128]{3,2,1,0:T(1,128)}, u32[]{:S(2)}, u32[]{:S(2)}) collective-permute-start(f32[3,8,1,128]{3,2,1,0:T(1,128)S(1)} %get-tuple-element.93), channel_id=1, source_target_pairs={{1,0},{2,1},{3,2},{4,3},{5,4},{6,5},{7,6},{8,7},{9,8},{10,9},{11,1... | collective-permute-start | bytes 36872 | tf_op jit(solution)/shard_map/ppermute | solution.py:34
  20.1 10.4 %copy-start.18 = (pred[8]{0:T(512)(128)(4,1)}, pred[8]{0:T(512)(128)(4,1)S(1)}, u32[]{:S(2)}) copy-start(pred[8]{0:T(512)(128)(4,1)S(1)} %compare_and_fusion) | copy-start | bytes 28
  27.7 23.7 %copy-start.16 = (s32[8]{0:T(128)}, s32[8]{0:T(128)S(1)}, u32[]{:S(2)}) copy-start(s32[8]{0:T(128)S(1)} %multiply_add_fusion) | copy-start | bytes 100
  31.2 0.7 copy-start.1
  37.3 8.3 %all-to-all-start = ((bf16[8,2,259]{2,1,0:T(2,128)(2,1)}), bf16[8,2,259]{2,1,0:T(2,128)(2,1)S(1)}, u32[]{:S(2)}, u32[]{:S(2)}) async-start(bf16[8,2,259]{2,1,0:T(2,128)(2,1)} %pad_maximum_fusion.2), calls=%async_computation | async-start | bytes 24576 | tf_op jit(solution)/shard_map/all_to_all | solution.py:50
  40.7 60.5 %all-gather.6.cloned.1.call-start = ((), (), s32[]{:S(2)}) async-start(), calls=%async_computation.4 | async-start | bytes 1179648 | tf_op jit(solution)/shard_map/all_gather | solution.py:64
  45.9 12.5 %copy-start.12 = (f32[16]{0:T(128)}, f32[16]{0:T(128)S(1)}, u32[]{:S(2)}) copy-start(f32[16]{0:T(128)S(1)} %convert_reduce_fusion) | copy-start | bytes 196
  46.0 5.4 %copy-start.7 = (bf16[16,256]{0,1:T(8,128)(2,1)}, bf16[16,256]{0,1:T(8,128)(2,1)S(1)}, u32[]{:S(2)}) copy-start(bf16[16,256]{0,1:T(8,128)(2,1)S(1)} %copy.74) | copy-start | bytes 24580
  52.7 5.0 %copy-start.10 = (bf16[1,2048,2]{1,2,0:T(2,128)(2,1)S(1)}, bf16[1,2048,2]{1,2,0:T(2,128)(2,1)}, u32[]{:S(2)}) copy-start(bf16[1,2048,2]{1,2,0:T(2,128)(2,1)} %param.24) | copy-start | bytes 24580
  53.1 5.6 %copy-start.14 = (bf16[16,2]{0,1:T(2,128)(2,1)}, bf16[16,2]{0,1:T(2,128)(2,1)S(1)}, u32[]{:S(2)}) copy-start(bf16[16,2]{0,1:T(2,128)(2,1)S(1)} %copy.88) | copy-start | bytes 196
  53.1 12.7 %copy-start.2 = (f32[3,8,16,128]{3,2,1,0:T(8,128)S(1)}, f32[3,8,16,128]{3,2,1,0:T(8,128)}, u32[]{:S(2)}) copy-start(f32[3,8,16,128]{3,2,1,0:T(8,128)} %copy-done.1) | copy-start | bytes 589828
  57.7 0.6 copy-start.5
  64.1 279.2 %all-reduce.3.cloned.1.call-start = ((), (), s32[]{:S(2)}) async-start(), calls=%async_computation.3 | async-start | bytes 1769472 | tf_op jit(solution)/shard_map/psum | solution.py:282
  66.6 6.1 %copy-start.3 = (f32[16,4,4,8,64]{4,0,3,2,1:T(8,128)S(1)}, f32[16,4,4,8,64]{4,0,3,2,1:T(8,128)}, u32[]{:S(2)}) copy-start(f32[16,4,4,8,64]{4,0,3,2,1:T(8,128)} %get-tuple-element.98) | copy-start | bytes 1572868
  72.7 4.4 %copy-start.4 = (bf16[1,27,64,64]{3,2,1,0:T(8,128)(2,1)S(1)}, bf16[1,27,64,64]{3,2,1,0:T(8,128)(2,1)}, u32[]{:S(2)}) copy-start(bf16[1,27,64,64]{3,2,1,0:T(8,128)(2,1)} %param.22) | copy-start | bytes 663556
  72.7 4.4 %copy-start.8 = (bf16[16,256]{0,1:T(8,128)(2,1)S(1)}, bf16[16,256]{0,1:T(8,128)(2,1)}, u32[]{:S(2)}) copy-start(bf16[16,256]{0,1:T(8,128)(2,1)} %copy-done.7) | copy-start | bytes 24580
  76.8 24.4 %copy-start.6 = (bf16[16,2048]{1,0:T(8,128)(2,1)S(1)}, bf16[16,2048]{1,0:T(8,128)(2,1)}, u32[]{:S(2)}) copy-start(bf16[16,2048]{1,0:T(8,128)(2,1)} %copy-done.5) | copy-start | bytes 196612
  76.8 24.4 %copy-start.13 = (f32[16]{0:T(128)S(1)}, f32[16]{0:T(128)}, u32[]{:S(2)}) copy-start(f32[16]{0:T(128)} %copy-done.12) | copy-start | bytes 196
  76.8 24.4 %copy-start.15 = (bf16[16,2]{0,1:T(2,128)(2,1)S(1)}, bf16[16,2]{0,1:T(2,128)(2,1)}, u32[]{:S(2)}) copy-start(bf16[16,2]{0,1:T(2,128)(2,1)} %copy-done.14) | copy-start | bytes 196
  76.8 160.9 %copy-start.11 = (bf16[1,2048,2]{1,2,0:T(2,128)(2,1)S(1)}, bf16[1,2048,2]{1,2,0:T(2,128)(2,1)}, u32[]{:S(2)}) copy-start(bf16[1,2048,2]{1,2,0:T(2,128)(2,1)} %param.24) | copy-start | bytes 24580
  76.8 172.6 %copy-start.17 = (s32[8]{0:T(128)S(1)}, s32[8]{0:T(128)}, u32[]{:S(2)}) copy-start(s32[8]{0:T(128)} %copy-done.16) | copy-start | bytes 100
  76.8 270.3 %all-gather.8.cloned.1.call-start = ((), (), s32[]{:S(2)}) async-start(), calls=%async_computation.5 | async-start | bytes 3145728 | tf_op jit(solution)/shard_map/all_gather | solution.py:64
  102.0 137.1 %all-to-all-start.1 = ((f32[8,2,2]{1,2,0:T(2,128)}), f32[8,2,2]{1,2,0:T(2,128)S(1)}, u32[]{:S(2)}, u32[]{:S(2)}) async-start(f32[8,2,2]{1,2,0:T(2,128)} %copy.77), calls=%async_computation.1 | async-start | bytes 16384 | tf_op jit(solution)/shard_map/all_to_all | solution.py:266
  239.1 20.0 %all-to-all-start.2 = ((bf16[32,2,512]{2,1,0:T(2,128)(2,1)}), bf16[32,2,512]{2,1,0:T(2,128)(2,1)S(1)}, u32[]{:S(2)}, u32[]{:S(2)}) async-start(bf16[32,2,512]{2,1,0:T(2,128)(2,1)} %reshape.333), calls=%async_computation.2 | async-start | bytes 131072 | tf_op jit(solution)/shard_map/all_to_all | solution.py:271
Sparse Core Ops, SparseCore 0:
  64.2 36.9 all-gather.5
  103.1 19.9 all-gather.7
Sparse Core Ops, SparseCore 1:
  76.8 266.4 all-reduce.2
where the time goes:
time: 360 us; the launch traced here: 359 us
  blocking collectives  134 us (37%)
  waiting for transfers between devices  117 us (32%)
  matrix products  31 us (9%)
  starting transfers between devices  27.4 us (8%)
  between operations  16.8 us (5%)
  other arithmetic  16.6 us (5%)
  local copies, waits for them, and re-layouts  15.5 us (4%)
    psum x1, blocking collectives, body(): lax.psum((grad_one, grad_two, grad_out), STREAM)  129 us
    psum x1, waiting for transfers between devices, body(): lax.psum((grad_one, grad_two, grad_out), STREAM)  84 us
    all_gather x2, waiting for transfers between devices, gather_in_order(): tiles = lax.all_gather(tiles, axes[k])  19.8 us
    all_to_all x1, starting transfers between devices, body(): lax.all_to_all(features, STREAM, split_axis=1, concat_axis=0, tiled=True)  10.2 us
    all_to_all x1, waiting for transfers between devices, body(): lax.all_to_all(features, STREAM, split_axis=1, concat_axis=0, tiled=True)  8.98 us
    transpose x2, matrix products, conv_filter(): return jnp.moveaxis(taps, 0, 3)  7.83 us
  transfers between devices with their start and end apart: 10, of which 4 were waited for; matrix products, arithmetic and copies ran while one was open for 16% of the time, Pallas kernels for 0%

commit v1 on v0

--- a/solution.py
+++ b/solution.py
@@ -279,7 +279,9 @@
     )
     own_rows = lax.dynamic_slice_in_dim(w_hidden[0], flow_place * share_rows, share_rows, 0)
     new_w_hidden = row_update(own_rows, grad_hidden)[None]
-    grad_one, grad_two, grad_out = lax.psum((grad_one, grad_two, grad_out), STREAM)
+    grad_one, grad_two, grad_out = lax.psum(
+        lax.psum((grad_one, grad_two, grad_out), "stream_0"), ("stream_1", "stream_2")
+    )
     new_k_second = row_update(k_second[0], grad_two)
     new_k_first = row_update(k_first[0], grad_one)
     new_w_out = whole_update(w_out[0], grad_out)

time: 360 us -> 258 us (0.72)
  blocking collectives: 134 us -> 53.3 us
  waiting for transfers between devices: 117 us -> 100 us
    psum x1 -> x2, blocking collectives: 129 us -> 47.9 us  [the longest x1 24.9 us: body(): lax.psum(lax.psum((grad_one, grad_two, grad_out), 'stream_0'), ('stream_1...]
    psum x1 -> x2, waiting for transfers between devices: 84 us -> 52.2 us  [the longest x1 52.2 us: body(): lax.psum((grad_one, grad_two, grad_out), 'stream_0')]
    all_gather x2, waiting for transfers between devices: 19.8 us -> 32.9 us  [gather_in_order(): tiles = lax.all_gather(tiles, axes[k])]
  transfers between devices with their start and end apart: 10 -> 11, of which waited for: 4 -> 5; matrix products, arithmetic and copies ran while one was open for 16% -> 12% of each run, Pallas kernels for 0% -> 0%
where the time goes in v1:
time: 258 us; the launch traced here: 257 us
  waiting for transfers between devices  100 us (39%)
  blocking collectives  53.3 us (21%)
  matrix products  28.1 us (11%)
  starting transfers between devices  27.8 us (11%)
  other arithmetic  17.4 us (7%)
  local copies, waits for them, and re-layouts  15.5 us (6%)
  between operations  15.1 us (6%)
    psum x1, waiting for transfers between devices, body(): lax.psum((grad_one, grad_two, grad_out), 'stream_0')  52.2 us
    all_gather x2, waiting for transfers between devices, gather_in_order(): tiles = lax.all_gather(tiles, axes[k])  32.9 us
    psum x1, blocking collectives, body(): lax.psum(lax.psum((grad_one, grad_two, grad_out), 'stream_0'), ('stream_1...  24.9 us
    psum x1, blocking collectives, body(): lax.psum((grad_one, grad_two, grad_out), 'stream_0')  23 us
    all_to_all x1, waiting for transfers between devices, body(): lax.all_to_all(features, STREAM, split_axis=1, concat_axis=0, tiled=True)  8.98 us
    transpose x2, matrix products, conv_filter(): return jnp.moveaxis(taps, 0, 3)  8.93 us
    all_to_all x1, starting transfers between devices, body(): lax.all_to_all(features, STREAM, split_axis=1, concat_axis=0, tiled=True)  8.47 us
    ppermute x2, starting transfers between devices, extended(): lax.ppermute(last, axis, up)  8.39 us
  transfers between devices with their start and end apart: 11, of which 5 were waited for; matrix products, arithmetic and copies ran while one was open for 12% of the time, Pallas kernels for 0%

profile of v1, /device:TPU:1, one launch (start us, length us, event | category | flops | bytes accessed | tf_op | source)
XLA Modules:
  0.0 257.5 jit_solution(11953828679941460608)
XLA Ops:
  8.0 2.0 collective-permute-start.2
  10.0 2.3 collective-permute-start.3
  13.7 0.9 fusion.44
  14.6 1.5 fusion.23
  16.8 0.8 select_reduce_fusion
  18.3 1.2 reshape.297
  21.9 1.1 reshape.300
  25.0 3.3 %all-to-all-start = ((bf16[8,2,259]{2,1,0:T(2,128)(2,1)}), bf16[8,2,259]{2,1,0:T(2,128)(2,1)S(1)}, u32[]{:S(2)}, u32[]{:S(2)}) async-start(bf16[8,2,259]{2,1,0:T(2,128)(2,1)} %pad_maximum_fusion.2), calls=%async_computation | async-start | bytes 24576 | tf_op jit(solution)/shard_map/all_to_all | solution.py:50
  28.6 4.7 %all-to-all-done = bf16[8,2,259]{2,1,0:T(2,128)(2,1)S(1)} async-done(((bf16[8,2,259]{2,1,0:T(2,128)(2,1)}), bf16[8,2,259]{2,1,0:T(2,128)(2,1)S(1)}, u32[]{:S(2)}, u32[]{:S(2)}) %all-to-all-start) | async-done | bytes 8320 | tf_op jit(solution)/shard_map/all_to_all | solution.py:50
  34.8 0.9 convolution_multiply_fusion.4
  35.7 3.1 %fusion.14 = (f32[16,4,4,8,64]{4,0,3,2,1:T(8,128)S(1)}, f32[16,4,4,8,64]{4,0,3,2,1:T(8,128)}) fusion(bf16[3,3,3,64,64]{4,3,2,1,0:T(8,128)(2,1)S(1)} %bitcast.139, f32[16,4,4,8,64]{4,0,3,2,1:T(8,128)S(1)} %convolution_multiply_fusion.4), kind=kOutput, calls=%fused_computation.26 | convolution fusion | flops 289669120 | bytes 1794048 | tf_op jit(solution)/shard_map/conv_general_dilated | solution.py:130
  39.3 4.6 %multiply_convert_fusion.3 = (bf16[16,2048]{1,0:T(8,128)(2,1)S(1)}, f32[16,2048]{1,0:T(8,128)S(1)}) fusion(bf16[16,2048]{1,0:T(8,128)(2,1)S(1)} %convert_element_type.116, bf16[1,2048,2048]{2,1,0:T(8,128)(2,1)} %param.23), kind=kOutput, calls=%fused_computation.50 | convolution fusion | flops 134414336 | bytes 8650752 | tf_op jit(solution)/shard_map/dot_general | solution.py:164
  44.8 5.7 %fusion.8 = f32[16,2048]{1,0:T(8,128)S(1)} fusion(bf16[16,2048]{1,0:T(8,128)(2,1)S(1)} %fusion.11, bf16[1,2048,2048]{2,1,0:T(8,128)(2,1)} %param.23), kind=kOutput, calls=%fused_computation.9 | convolution fusion | flops 134250496 | bytes 8585216 | tf_op jit(solution)/shard_map/dot_general | solution.py:174
  51.4 3.6 %convolution_multiply_fusion.5 = f32[3,3,3,64,64]{4,3,2,1,0:T(8,128)} fusion(bf16[16,4,4,8,64]{4,0,3,2,1:T(8,128)(2,1)S(1)} %multiply_convert_fusion, f32[16,4,4,8,64]{4,0,3,2,1:T(8,128)S(1)} %convolution_multiply_fusion.4), kind=kOutput, calls=%fused_computation.16 | convolution fusion | flops 289124352 | bytes 1228800 | tf_op jit(solution)/shard_map/transpose | solution.py:144
  55.1 5.4 %all-gather = bf16[32,2048]{1,0:T(8,128)(2,1)} all-gather(bf16[16,2048]{1,0:T(8,128)(2,1)S(1)} %copy-done.5), channel_id=2, replica_groups=mesh['wall'=8,'stream_0'=8,'stream_1'=2,'stream_2'=2] {'stream_1'}, dimensions={0}, use_global_device_ids=true | all-gather | bytes 196608 | tf_op jit(solution)/shard_map/all_gather | solution.py:64
  61.2 6.4 %collective-permute-start = (f32[3,8,1,128]{3,2,1,0:T(1,128)}, f32[3,8,1,128]{3,2,1,0:T(1,128)}, u32[]{:S(2)}, u32[]{:S(2)}) collective-permute-start(f32[3,8,1,128]{3,2,1,0:T(1,128)} %get-tuple-element.96), channel_id=1, source_target_pairs={{0,1},{1,2},{2,3},{3,4},{4,5},{5,6},{6,7},{7,8},{8,9},{9,10},{10,1... | collective-permute-start | bytes 36872 | tf_op jit(solution)/shard_map/ppermute | solution.py:33
  69.2 1.3 slice_add_fusion.5
  71.3 1.4 collective-permute-done.1
  72.8 1.3 slice_add_fusion.4
  74.8 1.7 fusion.20
  76.5 52.2 %all-reduce.5.cloned.1.call-done = f32[27,64,64]{2,1,0:T(8,128)} async-done(((f32[27,64,64]{2,1,0:T(8,128)}), f32[27,64,64]{2,1,0:T(8,128)}) %all-reduce.5.cloned.1.call-update) | async-done | bytes 442384 | tf_op jit(solution)/shard_map/psum | solution.py:283
  128.9 5.3 %convolution_multiply_fusion.6 = f32[3,3,3,2,64]{4,3,2,1,0:T(2,128)S(1)} fusion(bf16[16,2,4,4,8]{0,4,3,2,1:T(8,128)(2,1)} %bitcast.141, bf16[16,4,4,8,64]{4,0,3,2,1:T(8,128)(2,1)S(1)} %multiply_convert_fusion, bf16[3,3,3,64,64]{4,3,2,1,0:T(8,128)(2,1)} %bitcast.138, f32[16,4,4,8,64]{4,0,3,2,1:T(8,128)S(1)} %convolution_multiply_fusion.4), kind=kOutput, calls=%fused_computation.20 | convolution fusion | flops 298683776 | bytes 1029632 | tf_op jit(solution)/shard_map/transpose | solution.py:144
  134.2 32.9 %all-gather.6.cloned.1.call-done = bf16[16,16,2048]{2,1,0:T(8,128)(2,1)} async-done(((bf16[2,16,2048]{2,1,0:T(8,128)(2,1)}), bf16[16,16,2048]{2,1,0:T(8,128)(2,1)}) %all-gather.6.cloned.1.call-update) | async-done | bytes 1048592 | tf_op jit(solution)/shard_map/all_gather | solution.py:64
  168.0 4.9 %all-to-all-start.1 = ((f32[8,2,2]{1,2,0:T(2,128)}), f32[8,2,2]{1,2,0:T(2,128)S(1)}, u32[]{:S(2)}, u32[]{:S(2)}) async-start(f32[8,2,2]{1,2,0:T(2,128)} %copy.77), calls=%async_computation.1 | async-start | bytes 16384 | tf_op jit(solution)/shard_map/all_to_all | solution.py:266
  172.9 23.0 %all-reduce = (f32[54,64]{1,0:T(8,128)S(1)}, f32[2048,2]{0,1:T(2,128)S(1)}) all-reduce(f32[54,64]{1,0:T(8,128)S(1)} %reshape.304, f32[2048,2]{0,1:T(2,128)S(1)} %convolution_multiply_fusion.1), channel_id=1, replica_groups=mesh['wall'=8,'stream_0'=8,'stream_1'=2,'stream_2'=2] {'stream_0'}, use_global_device_ids=true, to_apply=%region_5.6 | all-reduce | flops 7552 | bytes 60416 | tf_op jit(solution)/shard_map/psum | solution.py:283
  195.9 24.9 %all-reduce.1 = (f32[54,64]{1,0:T(8,128)S(1)}, f32[2048,2]{0,1:T(2,128)S(1)}) all-reduce(f32[54,64]{1,0:T(8,128)S(1)} %get-tuple-element.84, f32[2048,2]{0,1:T(2,128)S(1)} %get-tuple-element.85), channel_id=1, replica_groups=mesh['wall'=8,'stream_0'=8,'stream_1'=2,'stream_2'=2] {'stream_1','strea..., use_global_device_ids=true, to_apply=%region_6.7 | all-reduce | flops 7552 | bytes 60416 | tf_op jit(solution)/shard_map/psum | solution.py:282
  224.3 8.5 %all-to-all-start.2 = ((bf16[32,2,512]{2,1,0:T(2,128)(2,1)}), bf16[32,2,512]{2,1,0:T(2,128)(2,1)S(1)}, u32[]{:S(2)}, u32[]{:S(2)}) async-start(bf16[32,2,512]{2,1,0:T(2,128)(2,1)} %reshape.333), calls=%async_computation.2 | async-start | bytes 131072 | tf_op jit(solution)/shard_map/all_to_all | solution.py:271
  233.7 9.0 %all-to-all-done.2 = bf16[32,2,512]{2,1,0:T(2,128)(2,1)S(1)} async-done(((bf16[32,2,512]{2,1,0:T(2,128)(2,1)}), bf16[32,2,512]{2,1,0:T(2,128)(2,1)S(1)}, u32[]{:S(2)}, u32[]{:S(2)}) %all-to-all-start.2) | async-done | bytes 65568 | tf_op jit(solution)/shard_map/all_to_all | solution.py:271
  242.8 1.5 multiply_reduce_fusion
  244.3 2.4 fusion.15
  246.7 1.7 copy.82
  249.1 1.9 fusion.16
  (132 shorter events, 21.0 us)
Async XLA Ops:
  7.2 21.4 %copy-start.10 = (bf16[1,54,64]{2,1,0:T(8,128)(2,1)S(1)}, bf16[1,54,64]{2,1,0:T(8,128)(2,1)}, u32[]{:S(2)}) copy-start(bf16[1,54,64]{2,1,0:T(8,128)(2,1)} %param.21) | copy-start | bytes 20740
  7.2 28.5 %copy-start.2 = (bf16[1,27,64,64]{3,2,1,0:T(8,128)(2,1)S(1)}, bf16[1,27,64,64]{3,2,1,0:T(8,128)(2,1)}, u32[]{:S(2)}) copy-start(bf16[1,27,64,64]{3,2,1,0:T(8,128)(2,1)} %param.22) | copy-start | bytes 663556
  8.0 13.8 %collective-permute-start.2 = (f32[3,1,16,128]{3,2,1,0:T(8,128)S(1)}, f32[3,1,16,128]{3,2,1,0:T(8,128)S(1)}, u32[]{:S(2)}, u32[]{:S(2)}) collective-permute-start(f32[3,1,16,128]{3,2,1,0:T(8,128)S(1)} %get-tuple-element.98), channel_id=1, source_target_pairs={{0,32},{32,64},{64,96},{96,128},{128,160},{160,192},{192,224},{224... | collective-permute-start | bytes 73736 | tf_op jit(solution)/shard_map/ppermute | solution.py:33
  10.0 11.8 %collective-permute-start.3 = (f32[3,1,16,128]{3,2,1,0:T(8,128)S(1)}, f32[3,1,16,128]{3,2,1,0:T(8,128)S(1)}, u32[]{:S(2)}, u32[]{:S(2)}) collective-permute-start(f32[3,1,16,128]{3,2,1,0:T(8,128)S(1)} %get-tuple-element.97), channel_id=1, source_target_pairs={{32,0},{64,32},{96,64},{128,96},{160,128},{192,160},{224,192},{0,2... | collective-permute-start | bytes 73736 | tf_op jit(solution)/shard_map/ppermute | solution.py:34
  18.3 17.4 %copy-start.21 = (s32[8]{0:T(128)}, s32[8]{0:T(128)S(1)}, u32[]{:S(2)}) copy-start(s32[8]{0:T(128)S(1)} %multiply_add_fusion) | copy-start | bytes 100
  25.0 8.3 %all-to-all-start = ((bf16[8,2,259]{2,1,0:T(2,128)(2,1)}), bf16[8,2,259]{2,1,0:T(2,128)(2,1)S(1)}, u32[]{:S(2)}, u32[]{:S(2)}) async-start(bf16[8,2,259]{2,1,0:T(2,128)(2,1)} %pad_maximum_fusion.2), calls=%async_computation | async-start | bytes 24576 | tf_op jit(solution)/shard_map/all_to_all | solution.py:50
  28.3 100.4 %all-reduce.5.cloned.1.call-start = ((), (), s32[]{:S(2)}) async-start(), calls=%async_computation.3 | async-start | bytes 1769472 | tf_op jit(solution)/shard_map/psum | solution.py:283
  34.8 4.0 %copy-start.8 = (bf16[16,256]{0,1:T(8,128)(2,1)}, bf16[16,256]{0,1:T(8,128)(2,1)S(1)}, u32[]{:S(2)}) copy-start(bf16[16,256]{0,1:T(8,128)(2,1)S(1)} %copy.74) | copy-start | bytes 24580
  38.9 5.0 %copy-start.13 = (bf16[1,2048,2]{1,2,0:T(2,128)(2,1)S(1)}, bf16[1,2048,2]{1,2,0:T(2,128)(2,1)}, u32[]{:S(2)}) copy-start(bf16[1,2048,2]{1,2,0:T(2,128)(2,1)} %param.24) | copy-start | bytes 24580
  39.0 5.6 %copy-start.17 = (f32[16]{0:T(128)S(1)}, f32[16]{0:T(128)}, u32[]{:S(2)}) copy-start(f32[16]{0:T(128)} %convert_reduce_fusion) | copy-start | bytes 196
  39.3 5.5 %copy-start.19 = (bf16[16,2]{0,1:T(2,128)(2,1)}, bf16[16,2]{0,1:T(2,128)(2,1)S(1)}, u32[]{:S(2)}) copy-start(bf16[16,2]{0,1:T(2,128)(2,1)S(1)} %copy.88) | copy-start | bytes 196
  43.9 7.0 %copy-start.1 = (f32[16,4,4,8,64]{4,0,3,2,1:T(8,128)S(1)}, f32[16,4,4,8,64]{4,0,3,2,1:T(8,128)}, u32[]{:S(2)}) copy-start(f32[16,4,4,8,64]{4,0,3,2,1:T(8,128)} %get-tuple-element.100) | copy-start | bytes 1572868
  44.1 6.8 %copy-start.15 = (f32[16,2]{0,1:T(2,128)}, f32[16,2]{0,1:T(2,128)S(1)}, u32[]{:S(2)}) copy-start(f32[16,2]{0,1:T(2,128)S(1)} %convolution_multiply_fusion.7) | copy-start | bytes 388
  44.8 6.1 %copy-start.4 = (bf16[16,2048]{1,0:T(8,128)(2,1)}, bf16[16,2048]{1,0:T(8,128)(2,1)S(1)}, u32[]{:S(2)}) copy-start(bf16[16,2048]{1,0:T(8,128)(2,1)S(1)} %fusion.11) | copy-start | bytes 196612
  50.9 9.6 %copy-start = (f32[3,8,16,128]{3,2,1,0:T(8,128)S(1)}, f32[3,8,16,128]{3,2,1,0:T(8,128)}, u32[]{:S(2)}) copy-start(f32[3,8,16,128]{3,2,1,0:T(8,128)} %param.18) | copy-start | bytes 589828
  51.3 3.7 %copy-start.5 = (bf16[16,2048]{1,0:T(8,128)(2,1)S(1)}, bf16[16,2048]{1,0:T(8,128)(2,1)}, u32[]{:S(2)}) copy-start(bf16[16,2048]{1,0:T(8,128)(2,1)} %copy-done.4) | copy-start | bytes 196612
  51.3 16.2 %copy-start.12 = (f32[32,16,1,1]{0,1,3,2:T(8,128)S(1)}, f32[32,16,1,1]{0,1,3,2:T(8,128)}, u32[]{:S(2)}) copy-start(f32[32,16,1,1]{0,1,3,2:T(8,128)} %constant.248) | copy-start | bytes 6148
  51.4 16.7 %copy-start.9 = (f32[256,128,1,1]{1,0,3,2:T(8,128)S(1)}, f32[256,128,1,1]{1,0,3,2:T(8,128)}, u32[]{:S(2)}) copy-start(f32[256,128,1,1]{1,0,3,2:T(8,128)} %constant.250) | copy-start | bytes 393220
  55.0 112.1 %all-gather.6.cloned.1.call-start = ((), (), s32[]{:S(2)}) async-start(), calls=%async_computation.5 | async-start | bytes 1179648 | tf_op jit(solution)/shard_map/all_gather | solution.py:64
  60.5 182.3 %all-reduce.7.cloned.1.call-start = ((), (), s32[]{:S(2)}) async-start(), calls=%async_computation.4 | async-start | bytes 1769472 | tf_op jit(solution)/shard_map/psum | solution.py:282
  61.2 8.0 %collective-permute-start = (f32[3,8,1,128]{3,2,1,0:T(1,128)}, f32[3,8,1,128]{3,2,1,0:T(1,128)}, u32[]{:S(2)}, u32[]{:S(2)}) collective-permute-start(f32[3,8,1,128]{3,2,1,0:T(1,128)} %get-tuple-element.96), channel_id=1, source_target_pairs={{0,1},{1,2},{2,3},{3,4},{4,5},{5,6},{6,7},{7,8},{8,9},{9,10},{10,1... | collective-permute-start | bytes 36872 | tf_op jit(solution)/shard_map/ppermute | solution.py:33
  67.5 5.2 %collective-permute-start.1 = (f32[3,8,1,128]{3,2,1,0:T(1,128)}, f32[3,8,1,128]{3,2,1,0:T(1,128)}, u32[]{:S(2)}, u32[]{:S(2)}) collective-permute-start(f32[3,8,1,128]{3,2,1,0:T(1,128)} %get-tuple-element.95), channel_id=1, source_target_pairs={{1,0},{2,1},{3,2},{4,3},{5,4},{6,5},{7,6},{8,7},{9,8},{10,9},{11,1... | collective-permute-start | bytes 36872 | tf_op jit(solution)/shard_map/ppermute | solution.py:34
  128.7 38.4 %copy-start.7 = (bf16[16,2048]{1,0:T(8,128)(2,1)S(1)}, bf16[16,2048]{1,0:T(8,128)(2,1)}, u32[]{:S(2)}) copy-start(bf16[16,2048]{1,0:T(8,128)(2,1)} %copy-done.6) | copy-start | bytes 196612
  128.7 38.4 %copy-start.16 = (f32[16,2]{0,1:T(2,128)S(1)}, f32[16,2]{0,1:T(2,128)}, u32[]{:S(2)}) copy-start(f32[16,2]{0,1:T(2,128)} %copy-done.15) | copy-start | bytes 388
  128.8 38.4 %copy-start.18 = (f32[16]{0:T(128)S(1)}, f32[16]{0:T(128)}, u32[]{:S(2)}) copy-start(f32[16]{0:T(128)} %convert_reduce_fusion) | copy-start | bytes 196
  128.8 38.4 %copy-start.20 = (bf16[16,2]{0,1:T(2,128)(2,1)S(1)}, bf16[16,2]{0,1:T(2,128)(2,1)}, u32[]{:S(2)}) copy-start(bf16[16,2]{0,1:T(2,128)(2,1)} %copy-done.19) | copy-start | bytes 196
  128.8 94.2 %copy-start.14 = (bf16[1,2048,2]{1,2,0:T(2,128)(2,1)S(1)}, bf16[1,2048,2]{1,2,0:T(2,128)(2,1)}, u32[]{:S(2)}) copy-start(bf16[1,2048,2]{1,2,0:T(2,128)(2,1)} %param.24) | copy-start | bytes 24580
  128.8 104.1 %copy-start.22 = (s32[8]{0:T(128)S(1)}, s32[8]{0:T(128)}, u32[]{:S(2)}) copy-start(s32[8]{0:T(128)} %copy-done.21) | copy-start | bytes 100
  128.8 115.5 %copy-start.3 = (bf16[1,27,64,64]{3,2,1,0:T(8,128)(2,1)S(1)}, bf16[1,27,64,64]{3,2,1,0:T(8,128)(2,1)}, u32[]{:S(2)}) copy-start(bf16[1,27,64,64]{3,2,1,0:T(8,128)(2,1)} %param.22) | copy-start | bytes 663556
  128.8 117.9 %all-gather.8.cloned.1.call-start = ((), (), s32[]{:S(2)}) async-start(), calls=%async_computation.6 | async-start | bytes 3145728 | tf_op jit(solution)/shard_map/all_gather | solution.py:64
  168.0 56.4 %all-to-all-start.1 = ((f32[8,2,2]{1,2,0:T(2,128)}), f32[8,2,2]{1,2,0:T(2,128)S(1)}, u32[]{:S(2)}, u32[]{:S(2)}) async-start(f32[8,2,2]{1,2,0:T(2,128)} %copy.77), calls=%async_computation.1 | async-start | bytes 16384 | tf_op jit(solution)/shard_map/all_to_all | solution.py:266
  224.3 18.3 %all-to-all-start.2 = ((bf16[32,2,512]{2,1,0:T(2,128)(2,1)}), bf16[32,2,512]{2,1,0:T(2,128)(2,1)S(1)}, u32[]{:S(2)}, u32[]{:S(2)}) async-start(bf16[32,2,512]{2,1,0:T(2,128)(2,1)} %reshape.333), calls=%async_computation.2 | async-start | bytes 131072 | tf_op jit(solution)/shard_map/all_to_all | solution.py:271
  (2 other events, 4.1 us)
Sparse Core Ops, SparseCore 0:
  55.1 73.5 all-reduce.4
  130.6 36.3 all-gather.5
  169.9 53.2 all-reduce.6
  225.1 16.0 all-gather.7
